TPU v7x, 128 devices: a whole 4x4x4 slice. The times are simulated.
128 devices in a mesh: heads: 4 (over z_lo, core), seq: 32 (over z_hi, x, y).
Axes of the slice: x: 4, y: 4, z: 4 (z_hi: 2, z_lo: 2; z = z_hi * 2 + z_lo), core: 2. Of those that a mesh axis runs over, the one named last changes fastest.
Arguments:
- tokens: bfloat16 [1, 32768, 8192], P(None, 'seq', 'heads'), may hold values from -22 to 22, as said below
- w_query: bfloat16 [8192, 4096], P('seq', 'heads'), may hold values from -0.0625 to 0.0625
- w_key: bfloat16 [8192, 1024], P('seq', 'heads'), may hold values from -0.0625 to 0.0625
- w_value: bfloat16 [8192, 1024], P('seq', 'heads'), may hold values from -0.0625 to 0.0625
- memory_in: float32 [1, 8, 128, 128], P(None, 'heads'), may hold values from -300 to 300, as said below
- norm_in: float32 [1, 8, 128], P(None, 'heads'), may hold values from 16 to 64
- gate_logit: float32 [32], P('heads'), may hold values from -2 to 2
Outputs:
- mixed: bfloat16 [1, 32768, 4096], P(None, 'seq', 'heads')
Inputs may be any that keep to these rules, and one draw needn't show every extreme that they name: `tokens`: input activations; every segment of a sequence has its own common component. memory_in[b, g, i, j] equals norm_in[b, g, i] times a factor.
All inputs are finite; a program needn't handle non-finite values.
Results may differ from a plain program's by a relative error of at most 0.0084.
Values may be sent and summed in bfloat16 or wider, within the bound.
No kernel may reach another device: no remote copies, remote signals or barrier semaphores. Data moves between devices by JAX's collectives and lax.ppermute only.
A program may use at most 128 MiB of HBM per device.

v0:
```python
import jax
import jax.numpy as jnp
from jax import lax
from jax.sharding import PartitionSpec as P


def prefix(array, axis, join, neutral):
    place = lax.axis_index(axis)
    gathered = jax.tree.map(
        lambda a, kind: lax.all_gather(a.astype(kind), axis), array, (jnp.bfloat16, jnp.bfloat16)
    )
    state = jax.tree.map(lambda a, e: jnp.zeros_like(a) + jnp.asarray(e, a.dtype), array, neutral)

    def one(step, state):
        return join(
            state,
            jax.tree.map(
                lambda a, own: lax.dynamic_index_in_dim(a, step, 0, False).astype(own.dtype),
                gathered,
                array,
            ),
        )

    return lax.fori_loop(0, place, one, state)


def elu_plus(v):
    return jnp.where(v > 0, v + 1.0, jnp.exp(jnp.minimum(v, 0.0)))


def add_pair(first, second):
    return (first[0] + second[0], first[1] + second[1])


def carry_memory(keys, values, memory_in, norm_in):
    highest = lax.Precision.HIGHEST
    sk = elu_plus(keys.astype(jnp.float32))
    contrib = jnp.einsum("bsgi,bsgj->bgij", sk, values.astype(jnp.float32), precision=highest)
    zterm = jnp.sum(sk, axis=1)
    start_state = (jnp.zeros_like(contrib), jnp.zeros_like(zterm))
    before, zbefore = prefix((contrib, zterm), "seq", add_pair, start_state)
    return (memory_in + before, norm_in + zbefore)


def per_device(tokens, w_query, w_key, w_value, memory_in, norm_in, gate_logit):
    whole = lax.all_gather(tokens, "heads", axis=2, tiled=True)
    batch, seglen, width = whole.shape
    flat = whole.reshape(batch * seglen, width)
    kv_heads = memory_in.shape[1]
    head_size = memory_in.shape[2]
    q_heads = gate_logit.shape[0]
    group = q_heads // kv_heads
    pieces = (
        lax.all_gather(w_query, "seq", axis=0, tiled=True),
        lax.all_gather(w_key, "seq", axis=0, tiled=True),
        lax.all_gather(w_value, "seq", axis=0, tiled=True),
    )
    q_acc, k_acc, v_acc = tuple(
        (jnp.dot(flat, piece, preferred_element_type=jnp.float32) for piece in pieces)
    )
    keys = k_acc.astype(jnp.bfloat16).reshape(batch, seglen, kv_heads, head_size)
    values = v_acc.astype(jnp.bfloat16).reshape(batch, seglen, kv_heads, head_size)
    memory, znorm = carry_memory(keys, values, memory_in, norm_in)
    queries = q_acc.astype(jnp.bfloat16).reshape(batch, seglen, kv_heads, group, head_size)
    highest = lax.Precision.HIGHEST
    scale = 1.0 / head_size**0.5
    causal = jnp.arange(seglen)[:, None] >= jnp.arange(seglen)[None, :]
    shares = jax.nn.sigmoid(gate_logit).reshape(kv_heads, group)

    def per_head(items):
        q_one, k_one, v_one, mem_one, norm_one, share_one = items
        sq = elu_plus(q_one.astype(jnp.float32))
        numer = jnp.einsum("bsri,bij->bsrj", sq, mem_one, precision=highest)
        denom = jnp.einsum("bsri,bi->bsr", sq, norm_one, precision=highest)
        retrieved = numer / denom[..., None]
        scores = (
            jnp.einsum("bsrd,btd->brst", q_one, k_one, preferred_element_type=jnp.float32) * scale
        )
        scores = jnp.where(causal, scores, -jnp.inf)
        top = jnp.max(scores, axis=-1, keepdims=True)
        expo = jnp.exp(scores - top)
        weights = (expo / jnp.sum(expo, axis=-1, keepdims=True)).astype(jnp.bfloat16)
        local = jnp.einsum("brst,btd->bsrd", weights, v_one, preferred_element_type=jnp.float32)
        share = share_one[None, None, :, None]
        return (share * retrieved + (1.0 - share) * local).astype(jnp.bfloat16)

    outputs = lax.map(
        per_head,
        (
            jnp.moveaxis(queries, 2, 0),
            jnp.moveaxis(keys, 2, 0),
            jnp.moveaxis(values, 2, 0),
            jnp.moveaxis(memory, 1, 0),
            jnp.moveaxis(znorm, 1, 0),
            shares,
        ),
    )
    mixed = jnp.moveaxis(outputs, 0, 2)
    return mixed.reshape(batch, seglen, q_heads * head_size)


def solution(mesh):
    in_specs = (
        P(None, "seq", "heads"),
        P("seq", "heads"),
        P("seq", "heads"),
        P("seq", "heads"),
        P(None, "heads", None, None),
        P(None, "heads", None),
        P("heads"),
    )
    out_specs = P(None, "seq", "heads")
    return jax.shard_map(
        per_device, mesh=mesh, in_specs=in_specs, out_specs=out_specs, check_vma=False
    )
```

profile of v0, /device:TPU:0, one launch (start us, length us, event | category | flops | bytes accessed | tf_op | source)
XLA Modules:
  0.0 655.9 jit_solution(10097445246627818363)
XLA Ops:
  6.5 0.0 all-gather.11.cloned.1.call-start
  6.5 0.7 all-gather.11.cloned.1.call-update
  7.3 0.0 all-gather.7.cloned.1.call-start
  7.3 0.7 all-gather.7.cloned.1.call-update
  8.0 0.0 all-gather.13.cloned.1.call-start
  8.1 0.7 all-gather.13.cloned.1.call-update
  8.7 0.0 all-gather.15.cloned.1.call-start
  8.8 86.4 %all-gather.11.cloned.1.call-done = bf16[8192,256]{1,0:T(8,128)(2,1)} async-done(((bf16[256,256]{1,0:T(8,128)(2,1)}), bf16[8192,256]{1,0:T(8,128)(2,1)}) %all-gather.11.cloned.1.call-update) | async-done | bytes 4194320 | tf_op jit(solution)/shard_map/all_gather | solution.py:55
  95.1 147.6 %all-gather.7.cloned.1.call-done = bf16[1,1024,8192]{2,1,0:T(8,128)(2,1)} async-done(((bf16[1,1024,2048]{2,1,0:T(8,128)(2,1)}), bf16[1,1024,8192]{2,1,0:T(8,128)(2,1)}) %all-gather.7.cloned.1.call-update) | async-done | bytes 16777232 | tf_op jit(solution)/shard_map/all_gather | solution.py:46
  242.8 9.6 %fusion.67 = (bf16[256]{0:T(256)(128)(2,1)S(1)}, f32[1024,256]{0,1:T(8,128)S(1)}, bf16[1024,256]{0,1:T(8,128)(2,1)S(1)}) fusion(bf16[8192,256]{1,0:T(8,128)(2,1)} %all-gather.11.cloned.1.call-done, bf16[1,1024,8192]{2,1,0:T(8,128)(2,1)} %all-gather.7.cloned.1.call-done), kind=kOutput, calls=%fused_computation.72 | convolution fusion | flops 4296802304 | bytes 22544896 | tf_op jit(solution)/shard_map/dot_general | solution.py:59
  252.4 0.0 copy-start.6
  252.4 78.6 %all-gather.13.cloned.1.call-done = bf16[8192,256]{1,0:T(8,128)(2,1)} async-done(((bf16[256,256]{1,0:T(8,128)(2,1)}), bf16[8192,256]{1,0:T(8,128)(2,1)}) %all-gather.13.cloned.1.call-update) | async-done | bytes 4194320 | tf_op jit(solution)/shard_map/all_gather | solution.py:56
  331.0 9.4 %fusion.62 = bf16[1024,256]{0,1:T(8,128)(2,1)S(1)} fusion(bf16[8192,256]{1,0:T(8,128)(2,1)} %all-gather.13.cloned.1.call-done, bf16[1,1024,8192]{2,1,0:T(8,128)(2,1)} %all-gather.7.cloned.1.call-done), kind=kOutput, calls=%fused_computation.65 | convolution fusion | flops 4295229440 | bytes 21495808 | tf_op jit(solution)/shard_map/dot_general | solution.py:59
  340.3 0.0 copy-start.5
  340.3 0.0 copy-start.4
  340.3 1.3 convolution_convert_fusion
  341.6 0.0 all-gather.15.cloned.1.call-update
  341.6 0.0 all-gather.9.cloned.1.call-start
  341.7 0.5 all-gather.9.cloned.1.call-update
  342.2 0.0 copy-done.6
  342.2 0.1 reshape.159
  342.3 1.0 copy.22
  343.3 89.9 %all_gather.28 = bf16[32,1,2,128]{3,2,1,0:T(2,128)(2,1)S(1)} all-gather(bf16[1,1,2,128]{3,2,1,0:T(2,128)(2,1)S(1)} %bitcast.183), channel_id=1, replica_groups=mesh['heads'=4,'seq'=32] {'seq'}, dimensions={0}, use_global_device_ids=true | all-gather | bytes 16896 | tf_op jit(solution)/shard_map/all_gather | solution.py:10
  433.2 0.0 all-gather.15.cloned.1.call-done
  433.2 0.0 copy-done.5
  433.3 0.0 copy-done.4
  433.3 132.9 %all-gather.9.cloned.1.call-done = bf16[8192,1024]{1,0:T(8,128)(2,1)} async-done(((bf16[256,1024]{1,0:T(8,128)(2,1)}), bf16[8192,1024]{1,0:T(8,128)(2,1)}) %all-gather.9.cloned.1.call-update) | async-done | bytes 16777232 | tf_op jit(solution)/shard_map/all_gather | solution.py:54
  566.2 22.1 %fusion.56 = bf16[1024,1024]{0,1:T(8,128)(2,1)S(1)} fusion(bf16[8192,1024]{1,0:T(8,128)(2,1)} %all-gather.9.cloned.1.call-done, bf16[1,1024,8192]{2,1,0:T(8,128)(2,1)} %all-gather.7.cloned.1.call-done), kind=kOutput, calls=%fused_computation.60 | convolution fusion | flops 17180917760 | bytes 35651584 | tf_op jit(solution)/shard_map/dot_general | solution.py:59
  588.2 2.6 copy.18
  590.8 52.6 %while.24 = (s32[]{:T(128)}, bf16[2,1,1024,4,128]{4,2,3,1,0:T(8,128)(2,1)}, f32[2,4]{1,0:T(2,128)S(1)}, bf16[2,1,1024,4,128]{4,2,3,1,0:T(8,128)(2,1)}, f32[2,1,1...) while((s32[]{:T(128)}, ...), condition=%wide.region_6.7_spmd.clone, body=%wide.region_3.6_spmd.clone.sunk | while | flops 3018317824 | bytes 84629256 | solution.py:87
  590.8 0.0 copy-start.2
  590.9 0.8 copy-done.2
  591.6 0.3 iota_compare_fusion.2
  592.0 3.3 fusion.94
  595.2 0.6 copy.29
  595.8 4.6 fusion.93
  600.4 4.1 fusion.91
  604.5 0.0 copy-start
  604.5 0.0 copy-start.3
  604.6 3.6 fusion.92
  608.2 0.0 copy-done
  608.2 0.0 copy-done.3
  608.2 7.6 %fusion.95 = bf16[2,1,1024,4,128]{4,2,3,1,0:T(8,128)(2,1)S(1)} fusion(bf16[2,1,1024,4,128]{4,2,3,1,0:T(8,128)(2,1)S(1)} %copy-done, s32[]{:T(128)S(6)} %copy.42, f32[4,1024]{1,0:T(4,128)S(1)} %fusion.92, f32[4,1024]{1,0:T(4,128)S(1)} %get-tuple-element.246, f32[1024,1024,4]{1,0,2:T(8,128)S(1)} %get-tuple-element.245, ...), kind=kOutput, calls=%fused_computation.23.clone.1 | convolution fusion | flops 1097334784 | bytes 21284864 | tf_op jit(solution)/shard_map/while/body/eval_jaxpr/brst,btd->bsrd/dot_general | solution.py:83
  615.8 0.0 copy-start.1
  615.8 1.3 copy-done.1
  617.2 0.0 copy-start.2
  617.2 0.8 copy-done.2
  618.0 0.3 iota_compare_fusion.2
  618.3 3.3 fusion.94
  621.5 0.6 copy.29
  622.2 4.6 fusion.93
  626.8 4.1 fusion.91
  630.9 0.0 copy-start
  630.9 0.0 copy-start.3
  630.9 3.6 fusion.92
  634.5 0.0 copy-done
  634.5 0.0 copy-done.3
  634.5 7.6 %fusion.95 = bf16[2,1,1024,4,128]{4,2,3,1,0:T(8,128)(2,1)S(1)} fusion(bf16[2,1,1024,4,128]{4,2,3,1,0:T(8,128)(2,1)S(1)} %copy-done, s32[]{:T(128)S(6)} %copy.42, f32[4,1024]{1,0:T(4,128)S(1)} %fusion.92, f32[4,1024]{1,0:T(4,128)S(1)} %get-tuple-element.246, f32[1024,1024,4]{1,0,2:T(8,128)S(1)} %get-tuple-element.245, ...), kind=kOutput, calls=%fused_computation.23.clone.1 | convolution fusion | flops 1097334784 | bytes 21284864 | tf_op jit(solution)/shard_map/while/body/eval_jaxpr/brst,btd->bsrd/dot_general | solution.py:83
  642.2 0.0 copy-start.1
  642.2 1.3 copy-done.1
  643.5 3.2 copy.23
  646.7 2.7 reshape.165
  (9 shorter events, 0.1 us)
Async XLA Ops:
  6.5 88.6 %all-gather.11.cloned.1.call-start = ((), (), s32[]{:S(2)}) async-start(), calls=%async_computation.2 | async-start | bytes 4325376 | tf_op jit(solution)/shard_map/all_gather | solution.py:55
  7.3 235.5 %all-gather.7.cloned.1.call-start = ((), (), s32[]{:S(2)}) async-start(), calls=%async_computation | async-start | bytes 20971520 | tf_op jit(solution)/shard_map/all_gather | solution.py:46
  8.0 322.9 %all-gather.13.cloned.1.call-start = ((), (), s32[]{:S(2)}) async-start(), calls=%async_computation.3 | async-start | bytes 4325376 | tf_op jit(solution)/shard_map/all_gather | solution.py:56
  8.7 424.5 %all-gather.15.cloned.1.call-start = ((), (), s32[]{:S(2)}) async-start(), calls=%async_computation.4 | async-start | bytes 2162688 | tf_op jit(solution)/shard_map/all_gather | solution.py:10
  252.4 89.8 %copy-start.6 = (f32[8]{0:T(128)S(1)}, f32[8]{0:T(128)}, u32[]{:S(2)}) copy-start(f32[8]{0:T(128)} %param.17) | copy-start | bytes 100
  340.3 92.9 %copy-start.5 = (f32[1,2,128]{2,1,0:T(2,128)S(1)}, f32[1,2,128]{2,1,0:T(2,128)}, u32[]{:S(2)}) copy-start(f32[1,2,128]{2,1,0:T(2,128)} %param.16) | copy-start | bytes 3076
  340.3 92.9 %copy-start.4 = (f32[1,2,128,128]{3,2,1,0:T(8,128)S(1)}, f32[1,2,128,128]{3,2,1,0:T(8,128)}, u32[]{:S(2)}) copy-start(f32[1,2,128,128]{3,2,1,0:T(8,128)} %param.15) | copy-start | bytes 393220
  341.6 224.6 %all-gather.9.cloned.1.call-start = ((), (), s32[]{:S(2)}) async-start(), calls=%async_computation.1 | async-start | bytes 17301504 | tf_op jit(solution)/shard_map/all_gather | solution.py:54
  590.8 0.8 copy-start.2
  604.5 3.7 copy-start
  604.5 3.7 copy-start.3
  615.8 1.3 copy-start.1
  617.2 0.8 copy-start.2
  630.9 3.7 copy-start
  630.9 3.7 copy-start.3
  642.2 1.3 copy-start.1
Sparse Core Ops, SparseCore 0:
  10.4 84.6 all-gather.10
  96.8 145.9 all-gather.6
  245.8 85.0 all-gather.12
  341.7 68.5 all-gather.14
  413.3 152.8 all-gather.8
where the time goes:
time: 658 us; the launch traced here: 656 us
  waiting for transfers between devices  448 us (68%)
  blocking collectives  89.9 us (14%)
  matrix products  81.4 us (12%)
  local copies, waits for them, and re-layouts  15.1 us (2%)
  between operations  13.3 us (2%)
  other arithmetic  7.96 us (1%)
    all_gather x1, waiting for transfers between devices, per_device(): whole = lax.all_gather(tokens, 'heads', axis=2, tiled=True)  148 us
    all_gather x1, waiting for transfers between devices, per_device(): lax.all_gather(w_query, 'seq', axis=0, tiled=True)  133 us
    all_gather x1, blocking collectives, prefix(): lax.all_gather(a.astype(kind), axis)  89.9 us
    all_gather x1, waiting for transfers between devices, per_device(): lax.all_gather(w_key, 'seq', axis=0, tiled=True)  86.4 us
    all_gather x1, waiting for transfers between devices, per_device(): lax.all_gather(w_value, 'seq', axis=0, tiled=True)  78.6 us
    dot_general x3, matrix products, per_device(): jnp.dot(flat, piece, preferred_element_type=jnp.float32)  41 us
    dot_general x2, matrix products, per_head(): jnp.einsum('brst,btd->bsrd', weights, v_one, preferred_element_type=jnp.f...  15.2 us
  transfers between devices with their start and end apart: 5, of which 4 were waited for; matrix products, arithmetic and copies ran while one was open for 2% of the time, Pallas kernels for 0%

commit v1 on v0

v1 whole, which is shorter than its diff:
```python
import jax
import jax.numpy as jnp
from jax import lax
from jax.sharding import PartitionSpec as P


def elu_plus(v):
    return jnp.where(v > 0, v + 1.0, jnp.exp(jnp.minimum(v, 0.0)))


def swap(x, axis, size, flip):
    return lax.ppermute(x, axis, [(i, i ^ flip) for i in range(size)])


def per_device(tokens, w_query, w_key, w_value, memory_in, norm_in, gate_logit):
    n_heads_dev = 4
    me = lax.axis_index("heads")
    n_seq = lax.axis_size("seq")
    place = lax.axis_index("seq")
    batch, seglen, part = tokens.shape
    kv_heads = memory_in.shape[1]
    head_size = memory_in.shape[2]
    q_heads = gate_logit.shape[0]
    group = q_heads // kv_heads
    qcols = w_query.shape[1]
    kcols = w_key.shape[1]

    wall = jnp.concatenate([w_query, w_key, w_value], axis=1)
    wall = lax.all_gather(wall, "seq", axis=0, tiled=True)

    flat = tokens.reshape(batch * seglen, part)
    cross = swap(flat, "heads", n_heads_dev, 2)
    near = swap(flat, "heads", n_heads_dev, 1)
    far = swap(cross, "heads", n_heads_dev, 1)
    blocks = (flat, near, cross, far)
    acc = None
    for k, blk in enumerate(blocks):
        src = me ^ k
        rows = lax.dynamic_slice_in_dim(wall, src * part, part, axis=0)
        term = jnp.dot(blk, rows, preferred_element_type=jnp.float32)
        acc = term if acc is None else acc + term
    q_acc = acc[:, :qcols]
    k_acc = acc[:, qcols:qcols + kcols]
    v_acc = acc[:, qcols + kcols:]

    keys = k_acc.astype(jnp.bfloat16).reshape(batch, seglen, kv_heads, head_size)
    values = v_acc.astype(jnp.bfloat16).reshape(batch, seglen, kv_heads, head_size)
    highest = lax.Precision.HIGHEST
    sk = elu_plus(keys.astype(jnp.float32))
    contrib = jnp.einsum("bsgi,bsgj->bgij", sk, values.astype(jnp.float32), precision=highest)
    zterm = jnp.sum(sk, axis=1)
    packed = jnp.concatenate([contrib.reshape(-1), zterm.reshape(-1)]).astype(jnp.bfloat16)
    every = lax.all_gather(packed, "seq", axis=0, tiled=False)
    mask = (jnp.arange(n_seq) < place).astype(jnp.float32)
    before = jnp.einsum("s,sn->n", mask, every.astype(jnp.float32), precision=highest)
    nmem = contrib.size
    memory = memory_in + before[:nmem].reshape(contrib.shape)
    znorm = norm_in + before[nmem:].reshape(zterm.shape)

    queries = q_acc.astype(jnp.bfloat16).reshape(batch, seglen, kv_heads, group, head_size)
    scale = 1.0 / head_size**0.5
    causal = jnp.arange(seglen)[:, None] >= jnp.arange(seglen)[None, :]
    shares = jax.nn.sigmoid(gate_logit).reshape(kv_heads, group)

    def per_head(items):
        q_one, k_one, v_one, mem_one, norm_one, share_one = items
        sq = elu_plus(q_one.astype(jnp.float32))
        numer = jnp.einsum("bsri,bij->bsrj", sq, mem_one, precision=highest)
        denom = jnp.einsum("bsri,bi->bsr", sq, norm_one, precision=highest)
        retrieved = numer / denom[..., None]
        scores = (
            jnp.einsum("bsrd,btd->brst", q_one, k_one, preferred_element_type=jnp.float32) * scale
        )
        scores = jnp.where(causal, scores, -jnp.inf)
        top = jnp.max(scores, axis=-1, keepdims=True)
        expo = jnp.exp(scores - top)
        weights = (expo / jnp.sum(expo, axis=-1, keepdims=True)).astype(jnp.bfloat16)
        local = jnp.einsum("brst,btd->bsrd", weights, v_one, preferred_element_type=jnp.float32)
        share = share_one[None, None, :, None]
        return (share * retrieved + (1.0 - share) * local).astype(jnp.bfloat16)

    outputs = lax.map(
        per_head,
        (
            jnp.moveaxis(queries, 2, 0),
            jnp.moveaxis(keys, 2, 0),
            jnp.moveaxis(values, 2, 0),
            jnp.moveaxis(memory, 1, 0),
            jnp.moveaxis(znorm, 1, 0),
            shares,
        ),
    )
    mixed = jnp.moveaxis(outputs, 0, 2)
    return mixed.reshape(batch, seglen, q_heads * head_size)


def solution(mesh):
    in_specs = (
        P(None, "seq", "heads"),
        P("seq", "heads"),
        P("seq", "heads"),
        P("seq", "heads"),
        P(None, "heads", None, None),
        P(None, "heads", None),
        P("heads"),
    )
    out_specs = P(None, "seq", "heads")
    return jax.shard_map(
        per_device, mesh=mesh, in_specs=in_specs, out_specs=out_specs, check_vma=False
    )
```

time: 658 us -> 459 us (0.70)
  waiting for transfers between devices: 448 us -> 320 us
  blocking collectives: 89.9 us -> 0 us
  matrix products: 81.4 us -> 91.6 us
    all_gather x5 -> x2, waiting for transfers between devices: 445 us -> 194 us  [the longest x1 119 us: per_device(): wall = lax.all_gather(wall, 'seq', axis=0, tiled=True)]
    ppermute x0 -> x3, waiting for transfers between devices: none -> 126 us  [swap(): return lax.ppermute(x, axis, [(i, i ^ flip) for i in range(size)])]
    all_gather x1 -> x0, blocking collectives: 89.9 us -> none  [prefix(): lax.all_gather(a.astype(kind), axis)]
    dot_general x4 -> x6, matrix products: 42.3 us -> 50.3 us  [the longest x4 46.9 us: per_device(): term = jnp.dot(blk, rows, preferred_element_type=jnp.float32)]
    dot_general x2, matrix products: 15.2 us -> 22.5 us  [per_head(): jnp.einsum('brst,btd->bsrd', weights, v_one, preferred_element_type=jnp.f...]
  transfers between devices with their start and end apart: 5 -> 5, of which waited for: 4 -> 3; matrix products, arithmetic and copies ran while one was open for 2% -> 8% of each run, Pallas kernels for 0% -> 0%
where the time goes in v1:
time: 459 us
  waiting for transfers between devices  320 us (70%)
  matrix products  91.6 us (20%)
  local copies, waits for them, and re-layouts  20.2 us (4%)
  between operations  13.5 us (3%)
  other arithmetic  11.2 us (2%)
    ppermute x3, waiting for transfers between devices, swap(): return lax.ppermute(x, axis, [(i, i ^ flip) for i in range(size)])  126 us
    all_gather x1, waiting for transfers between devices, per_device(): wall = lax.all_gather(wall, 'seq', axis=0, tiled=True)  119 us
    all_gather x1, waiting for transfers between devices, per_device(): every = lax.all_gather(packed, 'seq', axis=0, tiled=False)  74.8 us
    dot_general x4, matrix products, per_device(): term = jnp.dot(blk, rows, preferred_element_type=jnp.float32)  46.9 us
    dot_general x2, matrix products, per_head(): jnp.einsum('brst,btd->bsrd', weights, v_one, preferred_element_type=jnp.f...  22.5 us
  transfers between devices with their start and end apart: 5, of which 3 were waited for; matrix products, arithmetic and copies ran while one was open for 8% of the time, Pallas kernels for 0%

profile of v1, /device:TPU:0, one launch (start us, length us, event | category | flops | bytes accessed | tf_op | source)
XLA Modules:
  0.0 458.7 jit_solution(12396725212979575411)
XLA Ops:
  6.5 0.0 all-gather.4.cloned.1.call-start
  6.5 2.1 pad_maximum_fusion
  8.6 0.0 all-gather.4.cloned.1.call-update
  8.7 0.0 all-gather.6.cloned.1.call-start
  8.7 2.1 collective-permute-start.1
  10.8 0.0 collective-permute-start
  10.8 125.9 %collective-permute-done.1 = bf16[1024,2048]{1,0:T(8,128)(2,1)} collective-permute-done((bf16[1024,2048]{1,0:T(8,128)(2,1)}, bf16[1024,2048]{1,0:T(8,128)(2,1)}, u32[]{:S(2)}, u32[]{:S(2)}) %collective-permute-start.1) | collective-permute-done | bytes 4194336 | tf_op jit(solution)/shard_map/ppermute | solution.py:12
  136.8 0.0 collective-permute-start.2
  136.8 119.0 %all-gather.4.cloned.1.call-done = bf16[8192,1536]{1,0:T(8,128)(2,1)} async-done(((bf16[256,1536]{1,0:T(8,128)(2,1)}), bf16[8192,1536]{1,0:T(8,128)(2,1)}) %all-gather.4.cloned.1.call-update) | async-done | bytes 25165840 | tf_op jit(solution)/shard_map/all_gather | solution.py:29
  255.8 11.9 %fusion.52 = f32[1536,1024]{1,0:T(8,128)} fusion(bf16[1024,2048]{1,0:T(8,128)(2,1)} %collective-permute-done.1, bf16[8192,1536]{1,0:T(8,128)(2,1)} %all-gather.4.cloned.1.call-done, s32[]{:T(128)S(6)} %select_n.41), kind=kOutput, calls=%fused_computation.55 | convolution fusion | flops 6442450944 | bytes 16777220 | tf_op jit(solution)/shard_map/dot_general | solution.py:40
  267.8 1.5 copy-done.9
  269.3 10.5 %fusion.56 = f32[1536,1024]{1,0:T(8,128)} fusion(bf16[8192,1536]{1,0:T(8,128)(2,1)S(1)} %copy-done.9, s32[]{:T(128)S(6)} %select_n.39, bf16[1,1024,2048]{2,1,0:T(8,128)(2,1)} %param.9), kind=kOutput, calls=%fused_computation.59 | convolution fusion | flops 6442450944 | bytes 16777220 | tf_op jit(solution)/shard_map/dot_general | solution.py:40
  279.8 0.0 collective-permute-done
  279.8 10.5 %fusion.54 = f32[1536,1024]{1,0:T(8,128)} fusion(bf16[1024,2048]{1,0:T(8,128)(2,1)} %collective-permute-done, bf16[8192,1536]{1,0:T(8,128)(2,1)S(1)} %copy-done.9, s32[]{:T(128)S(6)} %select_n.40), kind=kOutput, calls=%fused_computation.57 | convolution fusion | flops 6442450944 | bytes 16777220 | tf_op jit(solution)/shard_map/dot_general | solution.py:40
  290.3 0.0 collective-permute-done.2
  290.3 14.0 %fusion.60 = bf16[1024,1536]{0,1:T(8,128)(2,1)S(1)} fusion(bf16[1024,2048]{1,0:T(8,128)(2,1)} %collective-permute-done.2, bf16[8192,1536]{1,0:T(8,128)(2,1)} %all-gather.4.cloned.1.call-done, s32[]{:T(128)S(6)} %select_n.42, f32[1536,1024]{1,0:T(8,128)} %fusion.52, f32[1536,1024]{1,0:T(8,128)} %fusion.56, f32[1536,1024]{1,0:T(8,128)} %fusion.54), kind=kOutput, calls=%fused_computation.61 | convolution fusion | flops 6448742400 | bytes 32505860 | tf_op jit(solution)/shard_map/dot_general | solution.py:40
  304.3 0.0 copy-start.1
  304.3 0.0 copy-start.10
  304.3 0.4 fusion.69
  304.7 1.3 copy-done.1
  306.0 0.1 fusion.83
  306.1 0.6 convolution_convert_fusion
  306.8 0.8 maximum_bitcast_fusion
  307.5 0.0 all-gather.6.cloned.1.call-update
  307.6 0.0 copy-done.10
  307.6 0.1 reshape.164
  307.7 1.8 slice.34
  309.5 0.0 copy-start.8
  309.5 0.0 copy-start.7
  309.5 2.6 copy.24
  312.1 0.3 copy.27
  312.4 74.8 %all-gather.6.cloned.1.call-done = bf16[32,1,33024]{2,1,0:T(2,128)(2,1)} async-done(((bf16[1,1,33024]{2,1,0:T(2,128)(2,1)}), bf16[32,1,33024]{2,1,0:T(2,128)(2,1)}) %all-gather.6.cloned.1.call-update) | async-done | bytes 2113552 | tf_op jit(solution)/shard_map/all_gather | solution.py:53
  387.1 2.7 fusion.66
  389.9 0.0 copy-done.8
  389.9 0.0 copy-done.7
  389.9 56.0 %while.11 = (s32[]{:T(128)}, bf16[2,1,1024,4,128]{4,2,3,1,0:T(8,128)(2,1)}, f32[2,4]{1,0:T(2,128)S(1)}, bf16[2,1,1024,4,128]{4,2,3,1,0:T(8,128)(2,1)}, f32[2,1,1...) while((s32[]{:T(128)}, ...), condition=%wide.region_4.5_spmd.clone, body=%wide.region_1.4_spmd.clone.sunk | while | flops 3018317824 | bytes 147542896 | solution.py:82
  389.9 0.0 copy-start.3
  389.9 0.0 copy-start.5
  389.9 0.3 iota_compare_fusion.2
  390.3 4.0 fusion.106
  394.3 0.0 copy-done.3
  394.3 0.0 copy-done.5
  394.3 0.0 copy-start
  394.3 0.0 copy-start.2
  394.4 3.6 fusion.107
  398.0 2.6 copy-done
  400.6 0.0 copy-done.2
  400.6 2.0 fusion.109
  402.7 0.6 copy.41
  403.3 3.3 fusion.108
  406.7 0.0 copy-start.4
  406.7 0.0 copy-start.6
  406.7 12.2 %fusion.110 = bf16[2,1,1024,4,128]{4,2,3,1,0:T(8,128)(2,1)} fusion(bf16[2,1,1024,4,128]{4,2,3,1,0:T(8,128)(2,1)} %get-tuple-element.162, s32[]{:T(128)} %get-tuple-element.161, f32[4,1024]{1,0:T(4,128)S(1)} %fusion.107, f32[4,1024]{1,0:T(4,128)S(1)} %get-tuple-element.149, f32[1024,1024,4]{1,0,2:T(8,128)} %copy-done, ...), kind=kOutput, calls=%fused_computation.21.clone.1 | convolution fusion | flops 1097334784 | bytes 21283872 | tf_op jit(solution)/shard_map/while/body/eval_jaxpr/brst,btd->bsrd/dot_general | solution.py:78
  418.9 0.0 copy-start.5
  419.0 0.3 iota_compare_fusion.2
  419.3 4.0 fusion.106
  423.4 3.6 fusion.107
  427.0 2.6 copy-done
  429.6 2.0 fusion.109
  431.7 0.6 copy.41
  432.3 3.3 fusion.108
  435.7 10.2 %fusion.110 = bf16[2,1,1024,4,128]{4,2,3,1,0:T(8,128)(2,1)} fusion(bf16[2,1,1024,4,128]{4,2,3,1,0:T(8,128)(2,1)} %get-tuple-element.162, s32[]{:T(128)} %get-tuple-element.161, f32[4,1024]{1,0:T(4,128)S(1)} %fusion.107, f32[4,1024]{1,0:T(4,128)S(1)} %get-tuple-element.149, f32[1024,1024,4]{1,0,2:T(8,128)} %copy-done, ...), kind=kOutput, calls=%fused_computation.21.clone.1 | convolution fusion | flops 1097334784 | bytes 21283872 | tf_op jit(solution)/shard_map/while/body/eval_jaxpr/brst,btd->bsrd/dot_general | solution.py:78
  445.9 3.2 copy.28
  449.2 2.7 reshape.171
  (22 shorter events, 0.1 us)
Async XLA Ops:
  6.5 249.3 %all-gather.4.cloned.1.call-start = ((), (), s32[]{:S(2)}) async-start(), calls=%async_computation | async-start | bytes 25952256 | tf_op jit(solution)/shard_map/all_gather | solution.py:29
  8.7 378.5 %all-gather.6.cloned.1.call-start = ((), (), s32[]{:S(2)}) async-start(), calls=%async_computation.1 | async-start | bytes 4359168 | tf_op jit(solution)/shard_map/all_gather | solution.py:53
  8.7 128.1 %collective-permute-start.1 = (bf16[1024,2048]{1,0:T(8,128)(2,1)}, bf16[1024,2048]{1,0:T(8,128)(2,1)}, u32[]{:S(2)}, u32[]{:S(2)}) collective-permute-start(bf16[1024,2048]{1,0:T(8,128)(2,1)} %bitcast.172), channel_id=1, source_target_pairs={{0,64},{32,96},{64,0},{96,32},{1,65},{33,97},{65,1},{97,33},{2,66}... | collective-permute-start | bytes 12582920 | tf_op jit(solution)/shard_map/ppermute | solution.py:12
  10.8 269.0 %collective-permute-start = (bf16[1024,2048]{1,0:T(8,128)(2,1)}, bf16[1024,2048]{1,0:T(8,128)(2,1)}, u32[]{:S(2)}, u32[]{:S(2)}) collective-permute-start(bf16[1024,2048]{1,0:T(8,128)(2,1)} %bitcast.173), channel_id=1, source_target_pairs={{0,32},{32,0},{64,96},{96,64},{1,33},{33,1},{65,97},{97,65},{2,34}... | collective-permute-start | bytes 12582920 | tf_op jit(solution)/shard_map/ppermute | solution.py:12
  136.8 153.5 %collective-permute-start.2 = (bf16[1024,2048]{1,0:T(8,128)(2,1)}, bf16[1024,2048]{1,0:T(8,128)(2,1)}, u32[]{:S(2)}, u32[]{:S(2)}) collective-permute-start(bf16[1024,2048]{1,0:T(8,128)(2,1)} %collective-permute-done.1), channel_id=1, source_target_pairs={{0,32},{32,0},{64,96},{96,64},{1,33},{33,1},{65,97},{97,65},{2,34}... | collective-permute-start | bytes 12582920 | tf_op jit(solution)/shard_map/ppermute | solution.py:12
  255.8 13.5 %copy-start.9 = (bf16[8192,1536]{1,0:T(8,128)(2,1)S(1)}, bf16[8192,1536]{1,0:T(8,128)(2,1)}, u32[]{:S(2)}) copy-start(bf16[8192,1536]{1,0:T(8,128)(2,1)} %all-gather.4.cloned.1.call-done) | copy-start | bytes 75497472
  304.3 1.7 copy-start.1
  304.3 3.3 copy-start.10
  309.5 80.4 %copy-start.8 = (f32[1,2,128]{2,1,0:T(2,128)S(1)}, f32[1,2,128]{2,1,0:T(2,128)}, u32[]{:S(2)}) copy-start(f32[1,2,128]{2,1,0:T(2,128)} %param.14) | copy-start | bytes 3076
  309.5 80.4 %copy-start.7 = (f32[1,2,128,128]{3,2,1,0:T(8,128)S(1)}, f32[1,2,128,128]{3,2,1,0:T(8,128)}, u32[]{:S(2)}) copy-start(f32[1,2,128,128]{3,2,1,0:T(8,128)} %param.13) | copy-start | bytes 393220
  389.9 4.4 copy-start.3
  389.9 4.4 copy-start.5
  394.3 6.3 %copy-start = (f32[1024,1024,4]{1,0,2:T(8,128)}, f32[1024,1024,4]{1,0,2:T(8,128)S(1)}, u32[]{:S(2)}) copy-start(f32[1024,1024,4]{1,0,2:T(8,128)S(1)} %get-tuple-element.148) | copy-start | bytes 50331652 | tf_op jit(solution)/shard_map/while
  394.3 6.3 %copy-start.2 = (bf16[2,1,1024,4,128]{4,2,3,1,0:T(8,128)(2,1)S(1)}, bf16[2,1,1024,4,128]{4,2,3,1,0:T(8,128)(2,1)}, u32[]{:S(2)}) copy-start(bf16[2,1,1024,4,128]{4,2,3,1,0:T(8,128)(2,1)} %get-tuple-element.173) | copy-start | bytes 6291460 | tf_op jit(solution)/shard_map/while
  406.7 12.3 %copy-start.4 = (bf16[2,1,1024,128]{2,3,1,0:T(8,128)(2,1)S(1)}, bf16[2,1,1024,128]{2,3,1,0:T(8,128)(2,1)}, u32[]{:S(2)}) copy-start(bf16[2,1,1024,128]{2,3,1,0:T(8,128)(2,1)} %copy-done.3) | copy-start | bytes 1572868 | tf_op jit(solution)/shard_map/while
  406.7 12.3 %copy-start.6 = (bf16[2,1,1024,128]{3,2,1,0:T(8,128)(2,1)S(1)}, bf16[2,1,1024,128]{3,2,1,0:T(8,128)(2,1)}, u32[]{:S(2)}) copy-start(bf16[2,1,1024,128]{3,2,1,0:T(8,128)(2,1)} %copy-done.5) | copy-start | bytes 1572868 | tf_op jit(solution)/shard_map/while
  418.9 4.4 copy-start.3
  418.9 4.4 copy-start.5
  423.3 6.3 %copy-start = (f32[1024,1024,4]{1,0,2:T(8,128)}, f32[1024,1024,4]{1,0,2:T(8,128)S(1)}, u32[]{:S(2)}) copy-start(f32[1024,1024,4]{1,0,2:T(8,128)S(1)} %get-tuple-element.148) | copy-start | bytes 50331652 | tf_op jit(solution)/shard_map/while
  423.4 6.3 %copy-start.2 = (bf16[2,1,1024,4,128]{4,2,3,1,0:T(8,128)(2,1)S(1)}, bf16[2,1,1024,4,128]{4,2,3,1,0:T(8,128)(2,1)}, u32[]{:S(2)}) copy-start(bf16[2,1,1024,4,128]{4,2,3,1,0:T(8,128)(2,1)} %get-tuple-element.173) | copy-start | bytes 6291460 | tf_op jit(solution)/shard_map/while
  435.7 10.3 %copy-start.4 = (bf16[2,1,1024,128]{2,3,1,0:T(8,128)(2,1)S(1)}, bf16[2,1,1024,128]{2,3,1,0:T(8,128)(2,1)}, u32[]{:S(2)}) copy-start(bf16[2,1,1024,128]{2,3,1,0:T(8,128)(2,1)} %copy-done.3) | copy-start | bytes 1572868 | tf_op jit(solution)/shard_map/while
  435.7 10.3 %copy-start.6 = (bf16[2,1,1024,128]{3,2,1,0:T(8,128)(2,1)S(1)}, bf16[2,1,1024,128]{3,2,1,0:T(8,128)(2,1)}, u32[]{:S(2)}) copy-start(bf16[2,1,1024,128]{3,2,1,0:T(8,128)(2,1)} %copy-done.5) | copy-start | bytes 1572868 | tf_op jit(solution)/shard_map/while
Sparse Core Ops, SparseCore 0:
  10.3 245.4 all-gather.3
  307.7 79.3 all-gather.5
